TPU v7x, 512 devices: a whole 4x4x16 slice. The times are simulated.
512 devices in a mesh: dp: 16 (over z), row: 4 (over y), col: 8 (over x, core).
Axes of the slice: x: 4, y: 4, z: 16, core: 2. Of those that a mesh axis runs over, the one named last changes fastest.
Arguments:
- layer_input: bfloat16 [3072, 4096], P(('dp', 'col'), 'row'), may hold values from -6 to 6
- hidden_grad: bfloat16 [3072, 14336], P(('dp', 'row'), 'col'), may hold values from -6 to 6
- gate_slots: bfloat16 [4, 8, 48, 128, 128], P('row', 'col', 'dp'), may hold values from -0.125 to 0.125
- up_slots: bfloat16 [4, 8, 48, 128, 128], P('row', 'col', 'dp'), may hold values from -0.125 to 0.125
- block_mask: int32 [32, 112], replicated, may hold values from 0 to 1, as said below
Outputs:
- input_grad: bfloat16 [3072, 4096], P(('dp', 'col'), 'row')
- gate_slot_grad: float32 [4, 8, 48, 128, 128], P('row', 'col', 'dp')
- up_slot_grad: float32 [4, 8, 48, 128, 128], P('row', 'col', 'dp')
Inputs may be any that keep to these rules, and one draw needn't show every extreme that they name: `block_mask`: every tile of 8 x 14 blocks keeps between 24 and 48 blocks; some tile keeps exactly 48, which tile depends on the draw.
All inputs are finite; a program needn't handle non-finite values.
Results may differ from a plain program's by a relative error of at most 0.022.
Values may be sent and summed in bfloat16 or wider, within the bound.
No kernel may reach another device: no remote copies, remote signals or barrier semaphores. Data moves between devices by JAX's collectives and lax.ppermute only.
A program may use at most 64 MiB of HBM per device.

v0:
```python
import jax
import jax.numpy as jnp
from jax import lax
from jax.sharding import PartitionSpec as P

F32 = jnp.float32
BF16 = jnp.bfloat16


def _shift(x, axis, n, step):
    return lax.ppermute(x, axis, perm=[(i, (i + step) % n) for i in range(n)])


def ring_gather(x, axis, n):
    ahead = n // 2
    behind = n - 1 - ahead
    out = [None] * n
    out[0] = x
    fwd = x
    bwd = x
    for s in range(1, ahead + 1):
        fwd = _shift(fwd, axis, n, 1)
        out[(n - s) % n] = fwd
        if s <= behind:
            bwd = _shift(bwd, axis, n, -1)
            out[s] = bwd
    return out


def ring_sum_scatter(parts, axis, n):
    ahead = n // 2
    behind = n - 1 - ahead
    fwd = parts[ahead]
    bwd = parts[(n - behind) % n] if behind > 0 else None
    for s in range(1, ahead + 1):
        fwd = _shift(fwd, axis, n, 1)
        total = fwd.astype(F32) + parts[ahead - s].astype(F32)
        fwd = total.astype(BF16) if s < ahead else total
        if s <= behind:
            bwd = _shift(bwd, axis, n, -1)
            if s < behind:
                bwd = (bwd.astype(F32) + parts[(s - behind) % n].astype(F32)).astype(BF16)
    if bwd is None:
        return fwd
    return fwd + bwd.astype(F32)


def on_device(layer_input, hidden_grad, gate_slots, up_slots, block_mask):
    n_dp = lax.axis_size("dp")
    n_row = lax.axis_size("row")
    n_col = lax.axis_size("col")
    k_dp = lax.axis_index("dp")
    k_row = lax.axis_index("row")
    k_col = lax.axis_index("col")
    bs = gate_slots.shape[-1]
    per_dev = gate_slots.shape[2]
    cap = per_dev * n_dp
    feat = layer_input.shape[1]
    units = hidden_grad.shape[1]
    tile_rows = feat // bs
    tile_cols = units // bs
    tok = layer_input.shape[0] * n_col
    rows_per = tok // n_row
    cols_per = tok // n_col
    gate_all = lax.all_gather(
        gate_slots[0, 0].reshape(per_dev * bs, bs), "dp", axis=0, tiled=True
    ).reshape(cap, bs, bs)
    up_all = lax.all_gather(
        up_slots[0, 0].reshape(per_dev * bs, bs), "dp", axis=0, tiled=True
    ).reshape(cap, bs, bs)
    x_rel = jnp.stack(ring_gather(layer_input, "col", n_col))
    x_abs = jnp.roll(x_rel, k_col, axis=0).reshape(tok, tile_rows, bs)
    tile_mask = lax.dynamic_slice(
        block_mask, (k_row * tile_rows, k_col * tile_cols), (tile_rows, tile_cols)
    ).reshape(tile_rows * tile_cols)
    kept = tile_mask > 0
    position = jnp.cumsum(kept.astype(jnp.int32)) - 1
    q = jnp.arange(cap, dtype=jnp.int32)
    picks = kept[None, :] & (position[None, :] == q[:, None])
    onehot3 = picks.astype(BF16).reshape(cap, tile_rows, tile_cols)
    row_pick = jnp.sum(onehot3, axis=2)
    col_pick = jnp.sum(onehot3, axis=1)
    high = lax.Precision.HIGH
    x_pick = jnp.einsum("qr,trk->qtk", row_pick, x_abs, preferred_element_type=F32).astype(BF16)

    def pre_rows(weights):
        per_slot = jnp.einsum("qtk,qkn->qtn", x_pick, weights, preferred_element_type=F32)
        pre = jnp.einsum(
            "qc,qtn->ctn",
            col_pick.astype(F32),
            per_slot,
            precision=high,
            preferred_element_type=F32,
        ).astype(BF16)
        pre_roll = jnp.roll(pre.reshape(tile_cols, n_row, rows_per, bs), -k_row, axis=1)
        return ring_sum_scatter([pre_roll[:, m] for m in range(n_row)], "row", n_row)

    gate = pre_rows(gate_all)
    up = pre_rows(up_all)
    upstream = hidden_grad.astype(F32).reshape(rows_per, tile_cols, bs).transpose(1, 0, 2)
    sig = jax.nn.sigmoid(gate)
    gate_grad = (upstream * up * sig * (1.0 + gate * (1.0 - sig))).astype(BF16)
    up_grad = (upstream * gate * sig).astype(BF16)

    def grad_slots(grad_part):
        grad_rel = jnp.stack(ring_gather(grad_part, "row", n_row), axis=1)
        grad_abs = jnp.roll(grad_rel, k_row, axis=1).reshape(tile_cols, tok, bs)
        return jnp.einsum("qc,ctn->qtn", col_pick, grad_abs, preferred_element_type=F32).astype(
            BF16
        )

    def slot_grad(picked):
        slot_dw = jnp.einsum("qtk,qtn->qkn", x_pick, picked, preferred_element_type=F32).astype(
            BF16
        )
        total = lax.psum_scatter(
            slot_dw.reshape(cap * bs, bs), "dp", scatter_dimension=0, tiled=True
        )
        return (total.astype(F32) / n_dp).reshape(per_dev, bs, bs)[None, None]

    gate_pick = grad_slots(gate_grad)
    gate_out = slot_grad(gate_pick)
    up_pick = grad_slots(up_grad)
    up_out = slot_grad(up_pick)
    dx_slot = jnp.einsum("qtn,qkn->qtk", gate_pick, gate_all, preferred_element_type=F32)
    dx_slot = dx_slot + jnp.einsum("qtn,qkn->qtk", up_pick, up_all, preferred_element_type=F32)
    dx = jnp.einsum(
        "qr,qtk->rtk", row_pick.astype(F32), dx_slot, precision=high, preferred_element_type=F32
    ).astype(BF16)
    dx_roll = jnp.roll(dx.reshape(tile_rows, n_col, cols_per, bs), -k_col, axis=1)
    dx_sum = ring_sum_scatter([dx_roll[:, m] for m in range(n_col)], "col", n_col)
    input_grad = dx_sum.transpose(1, 0, 2).reshape(cols_per, feat).astype(BF16)
    return (input_grad, gate_out, up_out)


def solution(mesh):
    return jax.shard_map(
        on_device,
        mesh=mesh,
        in_specs=(
            P(("dp", "col"), "row"),
            P(("dp", "row"), "col"),
            P("row", "col", "dp", None, None),
            P("row", "col", "dp", None, None),
            P(),
        ),
        out_specs=(
            P(("dp", "col"), "row"),
            P("row", "col", "dp", None, None),
            P("row", "col", "dp", None, None),
        ),
        check_vma=False,
    )
```

profile of v0, /device:TPU:2, one launch (start us, length us, event | category | flops | bytes accessed | tf_op | source)
XLA Modules:
  0.0 373.9 jit_solution(405065625400467713)
XLA Ops:
  11.1 5.3 %collective-permute-start.1 = (bf16[24,1024]{1,0:T(8,128)(2,1)S(1)}, bf16[24,1024]{1,0:T(8,128)(2,1)S(1)}, u32[]{:S(2)}, u32[]{:S(2)}) collective-permute-start(bf16[24,1024]{1,0:T(8,128)(2,1)S(1)} %collective-permute-done), channel_id=1, source_target_pairs={{0,7},{1,0},{2,1},{3,2},{4,3},{5,4},{6,5},{7,6},{8,15},{9,8},{10,9... | collective-permute-start | bytes 147464 | tf_op jit(solution)/shard_map/ppermute | solution.py:11
  16.5 1.7 collective-permute-done.1
  18.2 1.8 collective-permute-start.2
  20.0 3.5 collective-permute-done.5
  23.5 3.5 collective-permute-done.6
  28.9 57.6 %all-gather.3.cloned.1.call-done = bf16[6144,128]{1,0:T(8,128)(2,1)} async-done(((bf16[384,128]{1,0:T(8,128)(2,1)}), bf16[6144,128]{1,0:T(8,128)(2,1)}) %all-gather.3.cloned.1.call-update) | async-done | bytes 1572880 | tf_op jit(solution)/shard_map/all_gather | solution.py:68
  86.5 2.2 fusion.23
  88.7 3.5 fusion.25
  93.3 3.4 collective-permute-start.7
  96.7 60.8 %all-gather.5.cloned.1.call-done = bf16[6144,128]{1,0:T(8,128)(2,1)} async-done(((bf16[384,128]{1,0:T(8,128)(2,1)}), bf16[6144,128]{1,0:T(8,128)(2,1)}) %all-gather.5.cloned.1.call-update) | async-done | bytes 1572880 | tf_op jit(solution)/shard_map/all_gather | solution.py:65
  157.5 2.2 fusion.21
  159.7 3.5 fusion.28
  164.4 3.5 collective-permute-start.10
  167.8 3.6 collective-permute-start.9
  171.4 3.6 collective-permute-start.12
  175.8 2.4 collective-permute-start.8
  179.0 2.2 collective-permute-start.11
  181.2 1.1 reshape.130
  182.3 2.6 collective-permute-done.8
  184.9 5.3 %collective-permute-done.11 = bf16[14,48,128]{2,0,1:T(8,128)(2,1)} collective-permute-done((bf16[14,48,128]{2,0,1:T(8,128)(2,1)}, bf16[14,48,128]{2,0,1:T(8,128)(2,1)}, u32[]{:S(2)}, u32[]{:S(2)}) %collective-permute-start.11) | collective-permute-done | bytes 172064 | tf_op jit(solution)/shard_map/ppermute | solution.py:11
  190.2 2.3 fusion.60
  192.5 1.9 collective-permute-start.14
  194.4 1.9 collective-permute-start.17
  196.3 5.1 %collective-permute-start.13 = (bf16[14,48,128]{2,0,1:T(8,128)(2,1)}, bf16[14,48,128]{2,0,1:T(8,128)(2,1)S(1)}, u32[]{:S(2)}, u32[]{:S(2)}) collective-permute-start(bf16[14,48,128]{2,0,1:T(8,128)(2,1)} %get-tuple-element.9), channel_id=1, source_target_pairs={{0,24},{8,0},{16,8},{24,16},{1,25},{9,1},{17,9},{25,17},{2,26},{10... | collective-permute-start | bytes 516104 | tf_op jit(solution)/shard_map/ppermute | solution.py:11
  201.5 3.9 %collective-permute-start.16 = (bf16[14,48,128]{2,0,1:T(8,128)(2,1)}, bf16[14,48,128]{2,0,1:T(8,128)(2,1)S(1)}, u32[]{:S(2)}, u32[]{:S(2)}) collective-permute-start(bf16[14,48,128]{2,0,1:T(8,128)(2,1)} %get-tuple-element.8), channel_id=1, source_target_pairs={{0,24},{8,0},{16,8},{24,16},{1,25},{9,1},{17,9},{25,17},{2,26},{10... | collective-permute-start | bytes 516104 | tf_op jit(solution)/shard_map/ppermute | solution.py:11
  205.4 1.9 collective-permute-start.15
  207.4 1.9 collective-permute-start.18
  209.3 4.8 %collective-permute-done.15 = bf16[14,48,128]{2,0,1:T(8,128)(2,1)S(1)} collective-permute-done((bf16[14,48,128]{2,0,1:T(8,128)(2,1)S(1)}, bf16[14,48,128]{2,0,1:T(8,128)(2,1)S(1)}, u32[]{:S(2)}, u32[]{:S(2)}) %collective-permute-start.15) | collective-permute-done | bytes 172064 | tf_op jit(solution)/shard_map/ppermute | solution.py:11
  214.2 2.1 collective-permute-done.18
  217.0 3.6 fusion.37
  221.4 2.5 fusion.16
  224.8 2.4 fusion.13
  227.2 1.4 copy-done.4
  228.6 2.9 fusion.11
  231.6 1.1 convolution_add_fusion
  232.7 3.4 fusion.31
  236.3 3.5 collective-permute-done.19
  239.9 1.7 collective-permute-start.23
  241.6 1.8 collective-permute-done.20
  243.4 3.5 collective-permute-done.21
  247.5 1.6 collective-permute-done.24
  249.1 3.1 collective-permute-start.25
  252.2 0.9 collective-permute-done.22
  253.1 0.9 collective-permute-done.25
  254.6 38.0 %reduce-scatter.5.cloned.1.call-done = bf16[384,128]{1,0:T(8,128)(2,1)} async-done(((bf16[6144,128]{1,0:T(8,128)(2,1)}), bf16[384,128]{1,0:T(8,128)(2,1)}) %reduce-scatter.5.cloned.1.call-update) | async-done | bytes 98320 | tf_op jit(solution)/shard_map/reduce_scatter | solution.py:116
  292.6 1.6 convert_multiply_fusion
  294.2 71.6 %reduce-scatter.3.cloned.1.call-done = bf16[384,128]{1,0:T(8,128)(2,1)} async-done(((bf16[6144,128]{1,0:T(8,128)(2,1)}), bf16[384,128]{1,0:T(8,128)(2,1)}) %reduce-scatter.3.cloned.1.call-update) | async-done | bytes 98320 | tf_op jit(solution)/shard_map/reduce_scatter | solution.py:116
  365.8 1.6 convert_multiply_fusion.1
  (93 shorter events, 13.2 us)
Async XLA Ops:
  7.2 79.3 %all-gather.3.cloned.1.call-start = ((), (), s32[]{:S(2)}) async-start(), calls=%async_computation.2 | async-start | bytes 1671168 | tf_op jit(solution)/shard_map/all_gather | solution.py:68
  7.9 149.6 %all-gather.5.cloned.1.call-start = ((), (), s32[]{:S(2)}) async-start(), calls=%async_computation.3 | async-start | bytes 1671168 | tf_op jit(solution)/shard_map/all_gather | solution.py:65
  7.9 3.1 collective-permute-start
  8.0 8.5 %collective-permute-start.3 = (bf16[24,1024]{1,0:T(8,128)(2,1)}, bf16[24,1024]{1,0:T(8,128)(2,1)S(1)}, u32[]{:S(2)}, u32[]{:S(2)}) collective-permute-start(bf16[24,1024]{1,0:T(8,128)(2,1)} %param.7), channel_id=1, source_target_pairs={{0,1},{1,2},{2,3},{3,4},{4,5},{5,6},{6,7},{7,0},{8,9},{9,10},{10,1... | collective-permute-start | bytes 147464 | tf_op jit(solution)/shard_map/ppermute | solution.py:11
  8.6 284.0 %reduce-scatter.5.cloned.1.call-start = ((), (), s32[]{:S(2)}) async-start(), calls=%async_computation.5 | async-start | bytes 1671168 | tf_op jit(solution)/shard_map/reduce_scatter | solution.py:116
  11.1 7.1 %collective-permute-start.1 = (bf16[24,1024]{1,0:T(8,128)(2,1)S(1)}, bf16[24,1024]{1,0:T(8,128)(2,1)S(1)}, u32[]{:S(2)}, u32[]{:S(2)}) collective-permute-start(bf16[24,1024]{1,0:T(8,128)(2,1)S(1)} %collective-permute-done), channel_id=1, source_target_pairs={{0,7},{1,0},{2,1},{3,2},{4,3},{5,4},{6,5},{7,6},{8,15},{9,8},{10,9... | collective-permute-start | bytes 147464 | tf_op jit(solution)/shard_map/ppermute | solution.py:11
  16.4 3.5 collective-permute-start.4
  18.2 5.3 %collective-permute-start.2 = (bf16[24,1024]{1,0:T(8,128)(2,1)S(1)}, bf16[24,1024]{1,0:T(8,128)(2,1)S(1)}, u32[]{:S(2)}, u32[]{:S(2)}) collective-permute-start(bf16[24,1024]{1,0:T(8,128)(2,1)S(1)} %collective-permute-done.1), channel_id=1, source_target_pairs={{0,7},{1,0},{2,1},{3,2},{4,3},{5,4},{6,5},{7,6},{8,15},{9,8},{10,9... | collective-permute-start | bytes 147464 | tf_op jit(solution)/shard_map/ppermute | solution.py:11
  20.0 3.5 collective-permute-start.5
  23.5 3.5 collective-permute-start.6
  93.3 81.8 %collective-permute-start.7 = (bf16[14,48,128]{2,0,1:T(8,128)(2,1)S(1)}, bf16[14,48,128]{2,0,1:T(8,128)(2,1)S(1)}, u32[]{:S(2)}, u32[]{:S(2)}) collective-permute-start(bf16[14,48,128]{2,0,1:T(8,128)(2,1)S(1)} %get-tuple-element.12), channel_id=1, source_target_pairs={{0,8},{8,16},{16,24},{24,0},{1,9},{9,17},{17,25},{25,1},{2,10},{10... | collective-permute-start | bytes 516104 | tf_op jit(solution)/shard_map/ppermute | solution.py:11
  163.6 14.6 %copy-start.5 = (bf16[14,4,48,128]{3,0,2,1:T(8,128)(2,1)}, bf16[14,4,48,128]{3,0,2,1:T(8,128)(2,1)S(1)}, u32[]{:S(2)}) copy-start(bf16[14,4,48,128]{3,0,2,1:T(8,128)(2,1)S(1)} %fusion.48) | copy-start | bytes 2064388
  164.4 13.8 %collective-permute-start.10 = (bf16[14,48,128]{2,0,1:T(8,128)(2,1)S(1)}, bf16[14,48,128]{2,0,1:T(8,128)(2,1)S(1)}, u32[]{:S(2)}, u32[]{:S(2)}) collective-permute-start(bf16[14,48,128]{2,0,1:T(8,128)(2,1)S(1)} %get-tuple-element.10), channel_id=1, source_target_pairs={{0,8},{8,16},{16,24},{24,0},{1,9},{9,17},{17,25},{25,1},{2,10},{10... | collective-permute-start | bytes 516104 | tf_op jit(solution)/shard_map/ppermute | solution.py:11
  167.8 14.4 %collective-permute-start.9 = (bf16[14,48,128]{2,0,1:T(8,128)(2,1)}, bf16[14,48,128]{2,0,1:T(8,128)(2,1)}, u32[]{:S(2)}, u32[]{:S(2)}) collective-permute-start(bf16[14,48,128]{2,0,1:T(8,128)(2,1)} %get-tuple-element.13), channel_id=1, source_target_pairs={{0,24},{8,0},{16,8},{24,16},{1,25},{9,1},{17,9},{25,17},{2,26},{10... | collective-permute-start | bytes 516104 | tf_op jit(solution)/shard_map/ppermute | solution.py:11
  171.4 10.9 %collective-permute-start.12 = (bf16[14,48,128]{2,0,1:T(8,128)(2,1)}, bf16[14,48,128]{2,0,1:T(8,128)(2,1)}, u32[]{:S(2)}, u32[]{:S(2)}) collective-permute-start(bf16[14,48,128]{2,0,1:T(8,128)(2,1)} %get-tuple-element.11), channel_id=1, source_target_pairs={{0,24},{8,0},{16,8},{24,16},{1,25},{9,1},{17,9},{25,17},{2,26},{10... | collective-permute-start | bytes 516104 | tf_op jit(solution)/shard_map/ppermute | solution.py:11
  175.8 9.1 %collective-permute-start.8 = (bf16[14,48,128]{2,0,1:T(8,128)(2,1)}, bf16[14,48,128]{2,0,1:T(8,128)(2,1)}, u32[]{:S(2)}, u32[]{:S(2)}) collective-permute-start(bf16[14,48,128]{2,0,1:T(8,128)(2,1)} %fusion.58), channel_id=1, source_target_pairs={{0,8},{8,16},{16,24},{24,0},{1,9},{9,17},{17,25},{25,1},{2,10},{10... | collective-permute-start | bytes 516104 | tf_op jit(solution)/shard_map/ppermute | solution.py:11
  179.0 11.2 %collective-permute-start.11 = (bf16[14,48,128]{2,0,1:T(8,128)(2,1)}, bf16[14,48,128]{2,0,1:T(8,128)(2,1)}, u32[]{:S(2)}, u32[]{:S(2)}) collective-permute-start(bf16[14,48,128]{2,0,1:T(8,128)(2,1)} %fusion.52), channel_id=1, source_target_pairs={{0,8},{8,16},{16,24},{24,0},{1,9},{9,17},{17,25},{25,1},{2,10},{10... | collective-permute-start | bytes 516104 | tf_op jit(solution)/shard_map/ppermute | solution.py:11
  192.5 12.9 %collective-permute-start.14 = (bf16[14,48,128]{2,0,1:T(8,128)(2,1)}, bf16[14,48,128]{2,0,1:T(8,128)(2,1)S(1)}, u32[]{:S(2)}, u32[]{:S(2)}) collective-permute-start(bf16[14,48,128]{2,0,1:T(8,128)(2,1)} %get-tuple-element.9), channel_id=1, source_target_pairs={{0,8},{8,16},{16,24},{24,0},{1,9},{9,17},{17,25},{25,1},{2,10},{10... | collective-permute-start | bytes 516104 | tf_op jit(solution)/shard_map/ppermute | solution.py:11
  194.4 12.9 %collective-permute-start.17 = (bf16[14,48,128]{2,0,1:T(8,128)(2,1)}, bf16[14,48,128]{2,0,1:T(8,128)(2,1)S(1)}, u32[]{:S(2)}, u32[]{:S(2)}) collective-permute-start(bf16[14,48,128]{2,0,1:T(8,128)(2,1)} %get-tuple-element.8), channel_id=1, source_target_pairs={{0,8},{8,16},{16,24},{24,0},{1,9},{9,17},{17,25},{25,1},{2,10},{10... | collective-permute-start | bytes 516104 | tf_op jit(solution)/shard_map/ppermute | solution.py:11
  196.3 13.0 %collective-permute-start.13 = (bf16[14,48,128]{2,0,1:T(8,128)(2,1)}, bf16[14,48,128]{2,0,1:T(8,128)(2,1)S(1)}, u32[]{:S(2)}, u32[]{:S(2)}) collective-permute-start(bf16[14,48,128]{2,0,1:T(8,128)(2,1)} %get-tuple-element.9), channel_id=1, source_target_pairs={{0,24},{8,0},{16,8},{24,16},{1,25},{9,1},{17,9},{25,17},{2,26},{10... | collective-permute-start | bytes 516104 | tf_op jit(solution)/shard_map/ppermute | solution.py:11
  201.5 7.8 %collective-permute-start.16 = (bf16[14,48,128]{2,0,1:T(8,128)(2,1)}, bf16[14,48,128]{2,0,1:T(8,128)(2,1)S(1)}, u32[]{:S(2)}, u32[]{:S(2)}) collective-permute-start(bf16[14,48,128]{2,0,1:T(8,128)(2,1)} %get-tuple-element.8), channel_id=1, source_target_pairs={{0,24},{8,0},{16,8},{24,16},{1,25},{9,1},{17,9},{25,17},{2,26},{10... | collective-permute-start | bytes 516104 | tf_op jit(solution)/shard_map/ppermute | solution.py:11
  205.4 8.8 %collective-permute-start.15 = (bf16[14,48,128]{2,0,1:T(8,128)(2,1)S(1)}, bf16[14,48,128]{2,0,1:T(8,128)(2,1)S(1)}, u32[]{:S(2)}, u32[]{:S(2)}) collective-permute-start(bf16[14,48,128]{2,0,1:T(8,128)(2,1)S(1)} %collective-permute-done.14), channel_id=1, source_target_pairs={{0,8},{8,16},{16,24},{24,0},{1,9},{9,17},{17,25},{25,1},{2,10},{10... | collective-permute-start | bytes 516104 | tf_op jit(solution)/shard_map/ppermute | solution.py:11
  207.4 8.9 %collective-permute-start.18 = (bf16[14,48,128]{2,0,1:T(8,128)(2,1)S(1)}, bf16[14,48,128]{2,0,1:T(8,128)(2,1)S(1)}, u32[]{:S(2)}, u32[]{:S(2)}) collective-permute-start(bf16[14,48,128]{2,0,1:T(8,128)(2,1)S(1)} %collective-permute-done.17), channel_id=1, source_target_pairs={{0,8},{8,16},{16,24},{24,0},{1,9},{9,17},{17,25},{25,1},{2,10},{10... | collective-permute-start | bytes 516104 | tf_op jit(solution)/shard_map/ppermute | solution.py:11
  209.3 7.0 %copy-start.6 = (bf16[14,48,128]{2,0,1:T(8,128)(2,1)}, bf16[14,48,128]{2,0,1:T(8,128)(2,1)S(1)}, u32[]{:S(2)}) copy-start(bf16[14,48,128]{2,0,1:T(8,128)(2,1)S(1)} %collective-permute-done.13) | copy-start | bytes 516100
  209.3 7.0 %copy-start.7 = (bf16[14,48,128]{2,0,1:T(8,128)(2,1)}, bf16[14,48,128]{2,0,1:T(8,128)(2,1)S(1)}, u32[]{:S(2)}) copy-start(bf16[14,48,128]{2,0,1:T(8,128)(2,1)S(1)} %collective-permute-done.16) | copy-start | bytes 516100
  214.2 2.1 copy-start.8
  216.3 0.7 copy-start.9
  221.4 2.5 copy-start
  223.9 141.8 %reduce-scatter.3.cloned.1.call-start = ((), (), s32[]{:S(2)}) async-start(), calls=%async_computation.4 | async-start | bytes 1671168 | tf_op jit(solution)/shard_map/reduce_scatter | solution.py:116
  224.8 2.4 copy-start.2
  227.2 1.4 copy-start.4
  228.6 2.9 copy-start.1
  228.6 3.0 copy-start.3
  236.3 3.5 collective-permute-start.19
  239.9 3.5 collective-permute-start.20
  239.9 3.5 collective-permute-start.23
  243.4 3.5 collective-permute-start.21
  247.0 2.1 collective-permute-start.24
  247.3 5.8 %collective-permute-start.22 = (bf16[8,24,128]{2,0,1:T(8,128)(2,1)S(1)}, bf16[8,24,128]{2,0,1:T(8,128)(2,1)S(1)}, u32[]{:S(2)}, u32[]{:S(2)}) collective-permute-start(bf16[8,24,128]{2,0,1:T(8,128)(2,1)S(1)} %get-tuple-element.14), channel_id=1, source_target_pairs={{0,1},{1,2},{2,3},{3,4},{4,5},{5,6},{6,7},{7,0},{8,9},{9,10},{10,1... | collective-permute-start | bytes 147464 | tf_op jit(solution)/shard_map/ppermute | solution.py:11
  249.1 4.9 %collective-permute-start.25 = (bf16[8,24,128]{2,0,1:T(8,128)(2,1)S(1)}, bf16[8,24,128]{2,0,1:T(8,128)(2,1)S(1)}, u32[]{:S(2)}, u32[]{:S(2)}) collective-permute-start(bf16[8,24,128]{2,0,1:T(8,128)(2,1)S(1)} %fusion.61), channel_id=1, source_target_pairs={{0,7},{1,0},{2,1},{3,2},{4,3},{5,4},{6,5},{7,6},{8,15},{9,8},{10,9... | collective-permute-start | bytes 147464 | tf_op jit(solution)/shard_map/ppermute | solution.py:11
Sparse Core Ops, SparseCore 0:
  10.0 76.3 all-gather.2
  88.6 68.9 all-gather.4
  224.1 68.5 reduce-scatter.4
  295.3 70.4 reduce-scatter.2
where the time goes:
time: 375 us; the launch traced here: 374 us
  waiting for transfers between devices  265 us (71%)
  starting transfers between devices  48.7 us (13%)
  matrix products  26.1 us (7%)
  between operations  14.3 us (4%)
  other arithmetic  12.8 us (3%)
  local copies, waits for them, and re-layouts  7.4 us (2%)
    reduce_scatter x2, waiting for transfers between devices, slot_grad(): lax.psum_scatter(slot_dw.reshape(cap * bs, bs), 'dp', scatter_dimension=0...  110 us
    all_gather x1, waiting for transfers between devices, on_device(): lax.all_gather(gate_slots[0, 0].reshape(per_dev * bs, bs), 'dp', axis=0,...  60.8 us
    all_gather x1, waiting for transfers between devices, on_device(): lax.all_gather(up_slots[0, 0].reshape(per_dev * bs, bs), 'dp', axis=0, ti...  57.6 us
    ppermute x26, starting transfers between devices, _shift(): return lax.ppermute(x, axis, perm=[(i, (i + step) % n) for i in range(n)])  48.5 us
    ppermute x26, waiting for transfers between devices, _shift(): return lax.ppermute(x, axis, perm=[(i, (i + step) % n) for i in range(n)])  35.6 us
  transfers between devices with their start and end apart: 30, of which 17 were waited for; matrix products, arithmetic and copies ran while one was open for 9% of the time, Pallas kernels for 0%

commit v1 on v0

--- a/solution.py
+++ b/solution.py
@@ -5,6 +5,25 @@
 
 F32 = jnp.float32
 BF16 = jnp.bfloat16
+
+
+def gather_around(x, axis, dim):
+    size, mine, span = (lax.axis_size(axis), lax.axis_index(axis), x.shape[dim])
+    right = [(i, (i + 1) % size) for i in range(size)]
+    left = [(i, (i - 1) % size) for i in range(size)]
+    out = jnp.zeros((*x.shape[:dim], size * span, *x.shape[dim + 1 :]), x.dtype)
+    out = lax.dynamic_update_slice_in_dim(out, x, mine * span, axis=dim)
+    from_left = from_right = x
+    half = size // 2
+    for step in range(1, half + 1):
+        from_left = lax.ppermute(from_left, axis, right)
+        out = lax.dynamic_update_slice_in_dim(out, from_left, (mine - step) % size * span, axis=dim)
+        if step < size - half:
+            from_right = lax.ppermute(from_right, axis, left)
+            out = lax.dynamic_update_slice_in_dim(
+                out, from_right, (mine + step) % size * span, axis=dim
+            )
+    return out
 
 
 def _shift(x, axis, n, step):
@@ -62,9 +81,9 @@
     tok = layer_input.shape[0] * n_col
     rows_per = tok // n_row
     cols_per = tok // n_col
-    gate_all = lax.all_gather(
-        gate_slots[0, 0].reshape(per_dev * bs, bs), "dp", axis=0, tiled=True
-    ).reshape(cap, bs, bs)
+    gate_all = gather_around(gate_slots[0, 0].reshape(per_dev * bs, bs), "dp", 0).reshape(
+        cap, bs, bs
+    )
     up_all = lax.all_gather(
         up_slots[0, 0].reshape(per_dev * bs, bs), "dp", axis=0, tiled=True
     ).reshape(cap, bs, bs)

time: 375 us -> 323 us (0.86)
  the two profiles are of different devices: /device:TPU:2 before, /device:TPU:14 now
where the time goes in v1:
time: 323 us; the launch traced here: 322 us
  waiting for transfers between devices  145 us (45%)
  starting transfers between devices  115 us (36%)
  matrix products  24.7 us (8%)
  between operations  15 us (5%)
  other arithmetic  12.7 us (4%)
  local copies, waits for them, and re-layouts  10.3 us (3%)
    reduce_scatter x2, waiting for transfers between devices, slot_grad(): lax.psum_scatter(slot_dw.reshape(cap * bs, bs), 'dp', scatter_dimension=0...  112 us
    ppermute x26, starting transfers between devices, _shift(): return lax.ppermute(x, axis, perm=[(i, (i + step) % n) for i in range(n)])  55.7 us
    ppermute x7, starting transfers between devices, gather_around(): from_right = lax.ppermute(from_right, axis, left)  41.4 us
    ppermute x26, waiting for transfers between devices, _shift(): return lax.ppermute(x, axis, perm=[(i, (i + step) % n) for i in range(n)])  24 us
    ppermute x8, starting transfers between devices, gather_around(): from_left = lax.ppermute(from_left, axis, right)  17.2 us
    ppermute x8, waiting for transfers between devices, gather_around(): from_left = lax.ppermute(from_left, axis, right)  8.3 us
    dot_general x2, matrix products, pre_rows(): jnp.einsum('qc,qtn->ctn', col_pick.astype(F32), per_slot, precision=high,...  7.03 us
    unnamed x45, local copies, waits for them, and re-layouts  6.84 us
  transfers between devices with their start and end apart: 44, of which 19 were waited for; matrix products, arithmetic and copies ran while one was open for 10% of the time, Pallas kernels for 0%

profile of v1, /device:TPU:14, one launch (start us, length us, event | category | flops | bytes accessed | tf_op | source)
XLA Modules:
  0.0 322.0 jit_solution(14177289933173362368)
XLA Ops:
  7.2 3.8 %collective-permute-start.10 = (bf16[384,128]{1,0:T(8,128)(2,1)}, bf16[384,128]{1,0:T(8,128)(2,1)S(1)}, u32[]{:S(2)}, u32[]{:S(2)}) collective-permute-start(bf16[384,128]{1,0:T(8,128)(2,1)} %bitcast.166), channel_id=1, source_target_pairs={{0,32},{32,64},{64,96},{96,128},{128,160},{160,192},{192,224},{224... | collective-permute-start | bytes 294920 | tf_op jit(solution)/shard_map/ppermute | solution.py:19
  11.1 9.5 %collective-permute-start.11 = (bf16[384,128]{1,0:T(8,128)(2,1)}, bf16[384,128]{1,0:T(8,128)(2,1)S(1)}, u32[]{:S(2)}, u32[]{:S(2)}) collective-permute-start(bf16[384,128]{1,0:T(8,128)(2,1)} %bitcast.167), channel_id=1, source_target_pairs={{0,480},{32,0},{64,32},{96,64},{128,96},{160,128},{192,160},{224,1... | collective-permute-start | bytes 294920 | tf_op jit(solution)/shard_map/ppermute | solution.py:22
  26.2 1.9 collective-permute-start.12
  28.1 5.1 %collective-permute-start.13 = (bf16[384,128]{1,0:T(8,128)(2,1)S(1)}, bf16[384,128]{1,0:T(8,128)(2,1)S(1)}, u32[]{:S(2)}, u32[]{:S(2)}) collective-permute-start(bf16[384,128]{1,0:T(8,128)(2,1)S(1)} %collective-permute-done.11), channel_id=1, source_target_pairs={{0,480},{32,0},{64,32},{96,64},{128,96},{160,128},{192,160},{224,1... | collective-permute-start | bytes 294920 | tf_op jit(solution)/shard_map/ppermute | solution.py:22
  33.7 2.0 collective-permute-start.5
  37.2 2.6 collective-permute-start.6
  41.0 1.9 collective-permute-start.14
  42.9 5.1 %collective-permute-start.15 = (bf16[384,128]{1,0:T(8,128)(2,1)S(1)}, bf16[384,128]{1,0:T(8,128)(2,1)S(1)}, u32[]{:S(2)}, u32[]{:S(2)}) collective-permute-start(bf16[384,128]{1,0:T(8,128)(2,1)S(1)} %collective-permute-done.13), channel_id=1, source_target_pairs={{0,480},{32,0},{64,32},{96,64},{128,96},{160,128},{192,160},{224,1... | collective-permute-start | bytes 294920 | tf_op jit(solution)/shard_map/ppermute | solution.py:22
  50.7 1.9 collective-permute-start.16
  52.7 5.1 %collective-permute-start.17 = (bf16[384,128]{1,0:T(8,128)(2,1)S(1)}, bf16[384,128]{1,0:T(8,128)(2,1)S(1)}, u32[]{:S(2)}, u32[]{:S(2)}) collective-permute-start(bf16[384,128]{1,0:T(8,128)(2,1)S(1)} %collective-permute-done.15), channel_id=1, source_target_pairs={{0,480},{32,0},{64,32},{96,64},{128,96},{160,128},{192,160},{224,1... | collective-permute-start | bytes 294920 | tf_op jit(solution)/shard_map/ppermute | solution.py:22
  58.4 1.9 collective-permute-start.18
  60.4 5.5 %collective-permute-start.19 = (bf16[384,128]{1,0:T(8,128)(2,1)S(1)}, bf16[384,128]{1,0:T(8,128)(2,1)S(1)}, u32[]{:S(2)}, u32[]{:S(2)}) collective-permute-start(bf16[384,128]{1,0:T(8,128)(2,1)S(1)} %collective-permute-done.17), channel_id=1, source_target_pairs={{0,480},{32,0},{64,32},{96,64},{128,96},{160,128},{192,160},{224,1... | collective-permute-start | bytes 294920 | tf_op jit(solution)/shard_map/ppermute | solution.py:22
  66.4 1.9 collective-permute-start.20
  68.3 5.4 %collective-permute-start.21 = (bf16[384,128]{1,0:T(8,128)(2,1)S(1)}, bf16[384,128]{1,0:T(8,128)(2,1)S(1)}, u32[]{:S(2)}, u32[]{:S(2)}) collective-permute-start(bf16[384,128]{1,0:T(8,128)(2,1)S(1)} %collective-permute-done.19), channel_id=1, source_target_pairs={{0,480},{32,0},{64,32},{96,64},{128,96},{160,128},{192,160},{224,1... | collective-permute-start | bytes 294920 | tf_op jit(solution)/shard_map/ppermute | solution.py:22
  76.2 5.6 %collective-permute-start.23 = (bf16[384,128]{1,0:T(8,128)(2,1)S(1)}, bf16[384,128]{1,0:T(8,128)(2,1)S(1)}, u32[]{:S(2)}, u32[]{:S(2)}) collective-permute-start(bf16[384,128]{1,0:T(8,128)(2,1)S(1)} %collective-permute-done.21), channel_id=1, source_target_pairs={{0,480},{32,0},{64,32},{96,64},{128,96},{160,128},{192,160},{224,1... | collective-permute-start | bytes 294920 | tf_op jit(solution)/shard_map/ppermute | solution.py:22
  82.4 1.9 collective-permute-start.24
  84.3 6.3 %collective-permute-done.24 = bf16[384,128]{1,0:T(8,128)(2,1)S(1)} collective-permute-done((bf16[384,128]{1,0:T(8,128)(2,1)S(1)}, bf16[384,128]{1,0:T(8,128)(2,1)S(1)}, u32[]{:S(2)}, u32[]{:S(2)}) %collective-permute-start.24) | collective-permute-done | bytes 98336 | tf_op jit(solution)/shard_map/ppermute | solution.py:19
  91.4 3.5 %fusion.28 = bf16[14,192,128]{2,0,1:T(8,128)(2,1)S(1)} fusion(f32[48,192,128]{2,1,0:T(8,128)S(1)} %fusion.21, bf16[48,14]{0,1:T(8,128)(2,1)S(1)} %get-tuple-element.4), kind=kOutput, calls=%fused_computation.46 | convolution fusion | flops 99434496 | bytes 5408064 | tf_op jit(solution)/shard_map/qc,qtn->ctn/dot_general | solution.py:107
  96.0 3.7 %collective-permute-start.25 = (bf16[14,48,128]{2,0,1:T(8,128)(2,1)S(1)}, bf16[14,48,128]{2,0,1:T(8,128)(2,1)S(1)}, u32[]{:S(2)}, u32[]{:S(2)}) collective-permute-start(bf16[14,48,128]{2,0,1:T(8,128)(2,1)S(1)} %get-tuple-element.12), channel_id=1, source_target_pairs={{0,8},{8,16},{16,24},{24,0},{1,9},{9,17},{17,25},{25,1},{2,10},{10... | collective-permute-start | bytes 516104 | tf_op jit(solution)/shard_map/ppermute | solution.py:30
  99.7 2.3 collective-permute-start.27
  102.1 2.2 fusion.23
  104.3 3.5 %fusion.25 = bf16[14,192,128]{2,0,1:T(8,128)(2,1)S(1)} fusion(f32[48,192,128]{2,1,0:T(8,128)S(1)} %fusion.23, bf16[48,14]{0,1:T(8,128)(2,1)S(1)} %get-tuple-element.4), kind=kOutput, calls=%fused_computation.45 | convolution fusion | flops 99434496 | bytes 5408064 | tf_op jit(solution)/shard_map/qc,qtn->ctn/dot_general | solution.py:107
  108.9 3.7 %collective-permute-start.7 = (bf16[14,48,128]{2,0,1:T(8,128)(2,1)S(1)}, bf16[14,48,128]{2,0,1:T(8,128)(2,1)S(1)}, u32[]{:S(2)}, u32[]{:S(2)}) collective-permute-start(bf16[14,48,128]{2,0,1:T(8,128)(2,1)S(1)} %get-tuple-element.10), channel_id=1, source_target_pairs={{0,8},{8,16},{16,24},{24,0},{1,9},{9,17},{17,25},{25,1},{2,10},{10... | collective-permute-start | bytes 516104 | tf_op jit(solution)/shard_map/ppermute | solution.py:30
  113.4 3.3 %collective-permute-start.26 = (bf16[14,48,128]{2,0,1:T(8,128)(2,1)}, bf16[14,48,128]{2,0,1:T(8,128)(2,1)}, u32[]{:S(2)}, u32[]{:S(2)}) collective-permute-start(bf16[14,48,128]{2,0,1:T(8,128)(2,1)} %fusion.52), channel_id=1, source_target_pairs={{0,8},{8,16},{16,24},{24,0},{1,9},{9,17},{17,25},{25,1},{2,10},{10... | collective-permute-start | bytes 516104 | tf_op jit(solution)/shard_map/ppermute | solution.py:30
  116.8 2.5 collective-permute-start.9
  120.0 3.3 %collective-permute-start.8 = (bf16[14,48,128]{2,0,1:T(8,128)(2,1)}, bf16[14,48,128]{2,0,1:T(8,128)(2,1)}, u32[]{:S(2)}, u32[]{:S(2)}) collective-permute-start(bf16[14,48,128]{2,0,1:T(8,128)(2,1)} %fusion.58), channel_id=1, source_target_pairs={{0,8},{8,16},{16,24},{24,0},{1,9},{9,17},{17,25},{25,1},{2,10},{10... | collective-permute-start | bytes 516104 | tf_op jit(solution)/shard_map/ppermute | solution.py:30
  125.4 3.8 %collective-permute-done.8 = bf16[14,48,128]{2,0,1:T(8,128)(2,1)} collective-permute-done((bf16[14,48,128]{2,0,1:T(8,128)(2,1)}, bf16[14,48,128]{2,0,1:T(8,128)(2,1)}, u32[]{:S(2)}, u32[]{:S(2)}) %collective-permute-start.8) | collective-permute-done | bytes 172064 | tf_op jit(solution)/shard_map/ppermute | solution.py:30
  129.2 2.3 fusion.57
  131.5 2.5 collective-permute-start.29
  134.0 3.6 %collective-permute-start.32 = (bf16[14,48,128]{2,0,1:T(8,128)(2,1)}, bf16[14,48,128]{2,0,1:T(8,128)(2,1)S(1)}, u32[]{:S(2)}, u32[]{:S(2)}) collective-permute-start(bf16[14,48,128]{2,0,1:T(8,128)(2,1)} %get-tuple-element.9), channel_id=1, source_target_pairs={{0,8},{8,16},{16,24},{24,0},{1,9},{9,17},{17,25},{25,1},{2,10},{10... | collective-permute-start | bytes 516104 | tf_op jit(solution)/shard_map/ppermute | solution.py:30
  137.7 2.5 collective-permute-start.28
  140.2 5.1 %collective-permute-start.31 = (bf16[14,48,128]{2,0,1:T(8,128)(2,1)}, bf16[14,48,128]{2,0,1:T(8,128)(2,1)S(1)}, u32[]{:S(2)}, u32[]{:S(2)}) collective-permute-start(bf16[14,48,128]{2,0,1:T(8,128)(2,1)} %get-tuple-element.9), channel_id=1, source_target_pairs={{0,24},{8,0},{16,8},{24,16},{1,25},{9,1},{17,9},{25,17},{2,26},{10... | collective-permute-start | bytes 516104 | tf_op jit(solution)/shard_map/ppermute | solution.py:30
  145.4 1.9 collective-permute-start.30
  147.3 3.3 %collective-permute-start.33 = (bf16[14,48,128]{2,0,1:T(8,128)(2,1)S(1)}, bf16[14,48,128]{2,0,1:T(8,128)(2,1)S(1)}, u32[]{:S(2)}, u32[]{:S(2)}) collective-permute-start(bf16[14,48,128]{2,0,1:T(8,128)(2,1)S(1)} %collective-permute-done.32), channel_id=1, source_target_pairs={{0,8},{8,16},{16,24},{24,0},{1,9},{9,17},{17,25},{25,1},{2,10},{10... | collective-permute-start | bytes 516104 | tf_op jit(solution)/shard_map/ppermute | solution.py:30
  150.7 3.3 %collective-permute-done.30 = bf16[14,48,128]{2,0,1:T(8,128)(2,1)S(1)} collective-permute-done((bf16[14,48,128]{2,0,1:T(8,128)(2,1)S(1)}, bf16[14,48,128]{2,0,1:T(8,128)(2,1)S(1)}, u32[]{:S(2)}, u32[]{:S(2)}) %collective-permute-start.30) | collective-permute-done | bytes 172064 | tf_op jit(solution)/shard_map/ppermute | solution.py:30
  154.0 2.1 collective-permute-done.33
  156.8 3.5 %fusion.37 = (bf16[14,4,48,128]{3,0,2,1:T(8,128)(2,1)S(1)}, bf16[14,4,48,128]{3,0,2,1:T(8,128)(2,1)S(1)}) fusion(s32[]{:T(128)S(6)} %select_n.194, bf16[14,1,48,128]{3,0,2,1:T(8,128)(2,1)} %bitcast.30, bf16[14,1,48,128]{3,0,2,1:T(8,128)(2,1)} %bitcast.163, bf16[14,1,48,128]{3,0,2,1:T(8,128)(2,1)} %bitcast.165, bf16[14,1,48,128]{3,0,2,1:T(8,128)(2,1)S(1)} %bitcast.162, ...), kind=kLoop, calls=%fused_computation.51 | loop fusion | flops 4816896 | bytes 2752516 | tf_op jit(solution)/shard_map/jit(_roll_dynamic)/concatenate | solution.py:126
  162.5 2.4 fusion.16
  166.1 2.4 fusion.13
  169.9 2.9 fusion.8
  174.0 3.4 %fusion.31 = bf16[8,192,128]{2,0,1:T(8,128)(2,1)S(1)} fusion(f32[48,192,128]{2,1,0:T(8,128)S(1)} %convolution_add_fusion, bf16[48,8]{0,1:T(8,128)(2,1)S(1)} %get-tuple-element.5), kind=kOutput, calls=%fused_computation.47 | convolution fusion | flops 56819712 | bytes 5112576 | tf_op jit(solution)/shard_map/qr,qtk->rtk/dot_general | solution.py:146
  177.6 3.5 %collective-permute-done.34 = bf16[8,24,128]{2,0,1:T(8,128)(2,1)S(1)} collective-permute-done((bf16[8,24,128]{2,0,1:T(8,128)(2,1)S(1)}, bf16[8,24,128]{2,0,1:T(8,128)(2,1)S(1)}, u32[]{:S(2)}, u32[]{:S(2)}) %collective-permute-start.34) | collective-permute-done | bytes 49184 | tf_op jit(solution)/shard_map/ppermute | solution.py:30
  181.2 2.6 collective-permute-start.35
  184.7 3.8 %collective-permute-start.36 = (bf16[8,24,128]{2,0,1:T(8,128)(2,1)S(1)}, bf16[8,24,128]{2,0,1:T(8,128)(2,1)S(1)}, u32[]{:S(2)}, u32[]{:S(2)}) collective-permute-start(bf16[8,24,128]{2,0,1:T(8,128)(2,1)S(1)} %fusion.66), channel_id=1, source_target_pairs={{0,1},{1,2},{2,3},{3,4},{4,5},{5,6},{6,7},{7,0},{8,9},{9,10},{10,1... | collective-permute-start | bytes 147464 | tf_op jit(solution)/shard_map/ppermute | solution.py:30
  189.4 3.9 %collective-permute-start.37 = (bf16[8,24,128]{2,0,1:T(8,128)(2,1)S(1)}, bf16[8,24,128]{2,0,1:T(8,128)(2,1)S(1)}, u32[]{:S(2)}, u32[]{:S(2)}) collective-permute-start(bf16[8,24,128]{2,0,1:T(8,128)(2,1)S(1)} %get-tuple-element.14), channel_id=1, source_target_pairs={{0,1},{1,2},{2,3},{3,4},{4,5},{5,6},{6,7},{7,0},{8,9},{9,10},{10,1... | collective-permute-start | bytes 147464 | tf_op jit(solution)/shard_map/ppermute | solution.py:30
  194.1 5.2 %collective-permute-done.40 = bf16[8,24,128]{2,0,1:T(8,128)(2,1)S(1)} collective-permute-done((bf16[8,24,128]{2,0,1:T(8,128)(2,1)S(1)}, bf16[8,24,128]{2,0,1:T(8,128)(2,1)S(1)}, u32[]{:S(2)}, u32[]{:S(2)}) %collective-permute-start.40) | collective-permute-done | bytes 49184 | tf_op jit(solution)/shard_map/ppermute | solution.py:30
  200.0 40.6 %reduce-scatter.5.cloned.1.call-done = bf16[384,128]{1,0:T(8,128)(2,1)} async-done(((bf16[6144,128]{1,0:T(8,128)(2,1)}), bf16[384,128]{1,0:T(8,128)(2,1)}) %reduce-scatter.5.cloned.1.call-update) | async-done | bytes 98320 | tf_op jit(solution)/shard_map/reduce_scatter | solution.py:135
  242.1 71.7 %reduce-scatter.3.cloned.1.call-done = bf16[384,128]{1,0:T(8,128)(2,1)} async-done(((bf16[6144,128]{1,0:T(8,128)(2,1)}), bf16[384,128]{1,0:T(8,128)(2,1)}) %reduce-scatter.3.cloned.1.call-update) | async-done | bytes 98320 | tf_op jit(solution)/shard_map/reduce_scatter | solution.py:135
  (145 shorter events, 34.9 us)
Async XLA Ops:
  7.2 16.6 %copy-start.13 = (bf16[1,1,3,128,128]{4,3,2,1,0:T(8,128)(2,1)S(1)}, bf16[1,1,3,128,128]{4,3,2,1,0:T(8,128)(2,1)}, u32[]{:S(2)}) copy-start(bf16[1,1,3,128,128]{4,3,2,1,0:T(8,128)(2,1)} %param.9) | copy-start | bytes 294916
  7.2 94.9 %all-gather.2.cloned.1.call-start = ((), (), s32[]{:S(2)}) async-start(), calls=%async_computation.2 | async-start | bytes 1671168 | tf_op jit(solution)/shard_map/all_gather | solution.py:87
  7.2 19.0 %collective-permute-start.10 = (bf16[384,128]{1,0:T(8,128)(2,1)}, bf16[384,128]{1,0:T(8,128)(2,1)S(1)}, u32[]{:S(2)}, u32[]{:S(2)}) collective-permute-start(bf16[384,128]{1,0:T(8,128)(2,1)} %bitcast.166), channel_id=1, source_target_pairs={{0,32},{32,64},{64,96},{96,128},{128,160},{160,192},{192,224},{224... | collective-permute-start | bytes 294920 | tf_op jit(solution)/shard_map/ppermute | solution.py:19
  11.1 17.0 %collective-permute-start.11 = (bf16[384,128]{1,0:T(8,128)(2,1)}, bf16[384,128]{1,0:T(8,128)(2,1)S(1)}, u32[]{:S(2)}, u32[]{:S(2)}) collective-permute-start(bf16[384,128]{1,0:T(8,128)(2,1)} %bitcast.167), channel_id=1, source_target_pairs={{0,480},{32,0},{64,32},{96,64},{128,96},{160,128},{192,160},{224,1... | collective-permute-start | bytes 294920 | tf_op jit(solution)/shard_map/ppermute | solution.py:22
  20.6 3.5 %collective-permute-start = (bf16[24,1024]{1,0:T(8,128)(2,1)}, bf16[24,1024]{1,0:T(8,128)(2,1)S(1)}, u32[]{:S(2)}, u32[]{:S(2)}) collective-permute-start(bf16[24,1024]{1,0:T(8,128)(2,1)} %param.7), channel_id=1, source_target_pairs={{0,7},{1,0},{2,1},{3,2},{4,3},{5,4},{6,5},{7,6},{8,15},{9,8},{10,9... | collective-permute-start | bytes 147464 | tf_op jit(solution)/shard_map/ppermute | solution.py:30
  20.6 4.8 %collective-permute-start.3 = (bf16[24,1024]{1,0:T(8,128)(2,1)}, bf16[24,1024]{1,0:T(8,128)(2,1)S(1)}, u32[]{:S(2)}, u32[]{:S(2)}) collective-permute-start(bf16[24,1024]{1,0:T(8,128)(2,1)} %param.7), channel_id=1, source_target_pairs={{0,1},{1,2},{2,3},{3,4},{4,5},{5,6},{6,7},{7,0},{8,9},{9,10},{10,1... | collective-permute-start | bytes 147464 | tf_op jit(solution)/shard_map/ppermute | solution.py:30
  21.1 219.4 %reduce-scatter.5.cloned.1.call-start = ((), (), s32[]{:S(2)}) async-start(), calls=%async_computation.4 | async-start | bytes 1671168 | tf_op jit(solution)/shard_map/reduce_scatter | solution.py:135
  23.5 17.3 %copy-start.9 = (bf16[24,1024]{1,0:T(8,128)(2,1)S(1)}, bf16[24,1024]{1,0:T(8,128)(2,1)}, u32[]{:S(2)}) copy-start(bf16[24,1024]{1,0:T(8,128)(2,1)} %param.7) | copy-start | bytes 147460
  24.1 9.1 %collective-permute-start.1 = (bf16[24,1024]{1,0:T(8,128)(2,1)S(1)}, bf16[24,1024]{1,0:T(8,128)(2,1)S(1)}, u32[]{:S(2)}, u32[]{:S(2)}) collective-permute-start(bf16[24,1024]{1,0:T(8,128)(2,1)S(1)} %collective-permute-done), channel_id=1, source_target_pairs={{0,7},{1,0},{2,1},{3,2},{4,3},{5,4},{6,5},{7,6},{8,15},{9,8},{10,9... | collective-permute-start | bytes 147464 | tf_op jit(solution)/shard_map/ppermute | solution.py:30
  25.4 8.3 %collective-permute-start.4 = (bf16[24,1024]{1,0:T(8,128)(2,1)S(1)}, bf16[24,1024]{1,0:T(8,128)(2,1)S(1)}, u32[]{:S(2)}, u32[]{:S(2)}) collective-permute-start(bf16[24,1024]{1,0:T(8,128)(2,1)S(1)} %collective-permute-done.3), channel_id=1, source_target_pairs={{0,1},{1,2},{2,3},{3,4},{4,5},{5,6},{6,7},{7,0},{8,9},{9,10},{10,1... | collective-permute-start | bytes 147464 | tf_op jit(solution)/shard_map/ppermute | solution.py:30
  26.2 14.8 %collective-permute-start.12 = (bf16[384,128]{1,0:T(8,128)(2,1)S(1)}, bf16[384,128]{1,0:T(8,128)(2,1)S(1)}, u32[]{:S(2)}, u32[]{:S(2)}) collective-permute-start(bf16[384,128]{1,0:T(8,128)(2,1)S(1)} %collective-permute-done.10), channel_id=1, source_target_pairs={{0,32},{32,64},{64,96},{96,128},{128,160},{160,192},{192,224},{224... | collective-permute-start | bytes 294920 | tf_op jit(solution)/shard_map/ppermute | solution.py:19
  28.1 14.8 %collective-permute-start.13 = (bf16[384,128]{1,0:T(8,128)(2,1)S(1)}, bf16[384,128]{1,0:T(8,128)(2,1)S(1)}, u32[]{:S(2)}, u32[]{:S(2)}) collective-permute-start(bf16[384,128]{1,0:T(8,128)(2,1)S(1)} %collective-permute-done.11), channel_id=1, source_target_pairs={{0,480},{32,0},{64,32},{96,64},{128,96},{160,128},{192,160},{224,1... | collective-permute-start | bytes 294920 | tf_op jit(solution)/shard_map/ppermute | solution.py:22
  33.3 6.5 %collective-permute-start.2 = (bf16[24,1024]{1,0:T(8,128)(2,1)S(1)}, bf16[24,1024]{1,0:T(8,128)(2,1)S(1)}, u32[]{:S(2)}, u32[]{:S(2)}) collective-permute-start(bf16[24,1024]{1,0:T(8,128)(2,1)S(1)} %collective-permute-done.1), channel_id=1, source_target_pairs={{0,7},{1,0},{2,1},{3,2},{4,3},{5,4},{6,5},{7,6},{8,15},{9,8},{10,9... | collective-permute-start | bytes 147464 | tf_op jit(solution)/shard_map/ppermute | solution.py:30
  33.7 3.5 %collective-permute-start.5 = (bf16[24,1024]{1,0:T(8,128)(2,1)S(1)}, bf16[24,1024]{1,0:T(8,128)(2,1)S(1)}, u32[]{:S(2)}, u32[]{:S(2)}) collective-permute-start(bf16[24,1024]{1,0:T(8,128)(2,1)S(1)} %collective-permute-done.4), channel_id=1, source_target_pairs={{0,1},{1,2},{2,3},{3,4},{4,5},{5,6},{6,7},{7,0},{8,9},{9,10},{10,1... | collective-permute-start | bytes 147464 | tf_op jit(solution)/shard_map/ppermute | solution.py:30
  37.2 3.5 %collective-permute-start.6 = (bf16[24,1024]{1,0:T(8,128)(2,1)S(1)}, bf16[24,1024]{1,0:T(8,128)(2,1)S(1)}, u32[]{:S(2)}, u32[]{:S(2)}) collective-permute-start(bf16[24,1024]{1,0:T(8,128)(2,1)S(1)} %collective-permute-done.5), channel_id=1, source_target_pairs={{0,1},{1,2},{2,3},{3,4},{4,5},{5,6},{6,7},{7,0},{8,9},{9,10},{10,1... | collective-permute-start | bytes 147464 | tf_op jit(solution)/shard_map/ppermute | solution.py:30
  41.0 9.7 %collective-permute-start.14 = (bf16[384,128]{1,0:T(8,128)(2,1)S(1)}, bf16[384,128]{1,0:T(8,128)(2,1)S(1)}, u32[]{:S(2)}, u32[]{:S(2)}) collective-permute-start(bf16[384,128]{1,0:T(8,128)(2,1)S(1)} %collective-permute-done.12), channel_id=1, source_target_pairs={{0,32},{32,64},{64,96},{96,128},{128,160},{160,192},{192,224},{224... | collective-permute-start | bytes 294920 | tf_op jit(solution)/shard_map/ppermute | solution.py:19
  42.9 9.7 %collective-permute-start.15 = (bf16[384,128]{1,0:T(8,128)(2,1)S(1)}, bf16[384,128]{1,0:T(8,128)(2,1)S(1)}, u32[]{:S(2)}, u32[]{:S(2)}) collective-permute-start(bf16[384,128]{1,0:T(8,128)(2,1)S(1)} %collective-permute-done.13), channel_id=1, source_target_pairs={{0,480},{32,0},{64,32},{96,64},{128,96},{160,128},{192,160},{224,1... | collective-permute-start | bytes 294920 | tf_op jit(solution)/shard_map/ppermute | solution.py:22
  50.7 7.7 %collective-permute-start.16 = (bf16[384,128]{1,0:T(8,128)(2,1)S(1)}, bf16[384,128]{1,0:T(8,128)(2,1)S(1)}, u32[]{:S(2)}, u32[]{:S(2)}) collective-permute-start(bf16[384,128]{1,0:T(8,128)(2,1)S(1)} %collective-permute-done.14), channel_id=1, source_target_pairs={{0,32},{32,64},{64,96},{96,128},{128,160},{160,192},{192,224},{224... | collective-permute-start | bytes 294920 | tf_op jit(solution)/shard_map/ppermute | solution.py:19
  52.7 7.7 %collective-permute-start.17 = (bf16[384,128]{1,0:T(8,128)(2,1)S(1)}, bf16[384,128]{1,0:T(8,128)(2,1)S(1)}, u32[]{:S(2)}, u32[]{:S(2)}) collective-permute-start(bf16[384,128]{1,0:T(8,128)(2,1)S(1)} %collective-permute-done.15), channel_id=1, source_target_pairs={{0,480},{32,0},{64,32},{96,64},{128,96},{160,128},{192,160},{224,1... | collective-permute-start | bytes 294920 | tf_op jit(solution)/shard_map/ppermute | solution.py:22
  58.4 8.0 %collective-permute-start.18 = (bf16[384,128]{1,0:T(8,128)(2,1)S(1)}, bf16[384,128]{1,0:T(8,128)(2,1)S(1)}, u32[]{:S(2)}, u32[]{:S(2)}) collective-permute-start(bf16[384,128]{1,0:T(8,128)(2,1)S(1)} %collective-permute-done.16), channel_id=1, source_target_pairs={{0,32},{32,64},{64,96},{96,128},{128,160},{160,192},{192,224},{224... | collective-permute-start | bytes 294920 | tf_op jit(solution)/shard_map/ppermute | solution.py:19
  60.4 8.0 %collective-permute-start.19 = (bf16[384,128]{1,0:T(8,128)(2,1)S(1)}, bf16[384,128]{1,0:T(8,128)(2,1)S(1)}, u32[]{:S(2)}, u32[]{:S(2)}) collective-permute-start(bf16[384,128]{1,0:T(8,128)(2,1)S(1)} %collective-permute-done.17), channel_id=1, source_target_pairs={{0,480},{32,0},{64,32},{96,64},{128,96},{160,128},{192,160},{224,1... | collective-permute-start | bytes 294920 | tf_op jit(solution)/shard_map/ppermute | solution.py:22
  66.4 7.8 %collective-permute-start.20 = (bf16[384,128]{1,0:T(8,128)(2,1)S(1)}, bf16[384,128]{1,0:T(8,128)(2,1)S(1)}, u32[]{:S(2)}, u32[]{:S(2)}) collective-permute-start(bf16[384,128]{1,0:T(8,128)(2,1)S(1)} %collective-permute-done.18), channel_id=1, source_target_pairs={{0,32},{32,64},{64,96},{96,128},{128,160},{160,192},{192,224},{224... | collective-permute-start | bytes 294920 | tf_op jit(solution)/shard_map/ppermute | solution.py:19
  68.3 7.8 %collective-permute-start.21 = (bf16[384,128]{1,0:T(8,128)(2,1)S(1)}, bf16[384,128]{1,0:T(8,128)(2,1)S(1)}, u32[]{:S(2)}, u32[]{:S(2)}) collective-permute-start(bf16[384,128]{1,0:T(8,128)(2,1)S(1)} %collective-permute-done.19), channel_id=1, source_target_pairs={{0,480},{32,0},{64,32},{96,64},{128,96},{160,128},{192,160},{224,1... | collective-permute-start | bytes 294920 | tf_op jit(solution)/shard_map/ppermute | solution.py:22
  74.3 8.1 %collective-permute-start.22 = (bf16[384,128]{1,0:T(8,128)(2,1)S(1)}, bf16[384,128]{1,0:T(8,128)(2,1)S(1)}, u32[]{:S(2)}, u32[]{:S(2)}) collective-permute-start(bf16[384,128]{1,0:T(8,128)(2,1)S(1)} %collective-permute-done.20), channel_id=1, source_target_pairs={{0,32},{32,64},{64,96},{96,128},{128,160},{160,192},{192,224},{224... | collective-permute-start | bytes 294920 | tf_op jit(solution)/shard_map/ppermute | solution.py:19
  76.2 8.1 %collective-permute-start.23 = (bf16[384,128]{1,0:T(8,128)(2,1)S(1)}, bf16[384,128]{1,0:T(8,128)(2,1)S(1)}, u32[]{:S(2)}, u32[]{:S(2)}) collective-permute-start(bf16[384,128]{1,0:T(8,128)(2,1)S(1)} %collective-permute-done.21), channel_id=1, source_target_pairs={{0,480},{32,0},{64,32},{96,64},{128,96},{160,128},{192,160},{224,1... | collective-permute-start | bytes 294920 | tf_op jit(solution)/shard_map/ppermute | solution.py:22
  82.4 8.2 %collective-permute-start.24 = (bf16[384,128]{1,0:T(8,128)(2,1)S(1)}, bf16[384,128]{1,0:T(8,128)(2,1)S(1)}, u32[]{:S(2)}, u32[]{:S(2)}) collective-permute-start(bf16[384,128]{1,0:T(8,128)(2,1)S(1)} %collective-permute-done.22), channel_id=1, source_target_pairs={{0,32},{32,64},{64,96},{96,128},{128,160},{160,192},{192,224},{224... | collective-permute-start | bytes 294920 | tf_op jit(solution)/shard_map/ppermute | solution.py:19
  96.0 16.6 %collective-permute-start.25 = (bf16[14,48,128]{2,0,1:T(8,128)(2,1)S(1)}, bf16[14,48,128]{2,0,1:T(8,128)(2,1)S(1)}, u32[]{:S(2)}, u32[]{:S(2)}) collective-permute-start(bf16[14,48,128]{2,0,1:T(8,128)(2,1)S(1)} %get-tuple-element.12), channel_id=1, source_target_pairs={{0,8},{8,16},{16,24},{24,0},{1,9},{9,17},{17,25},{25,1},{2,10},{10... | collective-permute-start | bytes 516104 | tf_op jit(solution)/shard_map/ppermute | solution.py:30
  99.7 24.7 %collective-permute-start.27 = (bf16[14,48,128]{2,0,1:T(8,128)(2,1)}, bf16[14,48,128]{2,0,1:T(8,128)(2,1)}, u32[]{:S(2)}, u32[]{:S(2)}) collective-permute-start(bf16[14,48,128]{2,0,1:T(8,128)(2,1)} %get-tuple-element.13), channel_id=1, source_target_pairs={{0,24},{8,0},{16,8},{24,16},{1,25},{9,1},{17,9},{25,17},{2,26},{10... | collective-permute-start | bytes 516104 | tf_op jit(solution)/shard_map/ppermute | solution.py:30
  108.1 11.1 %copy-start.8 = (bf16[14,4,48,128]{3,0,2,1:T(8,128)(2,1)}, bf16[14,4,48,128]{3,0,2,1:T(8,128)(2,1)S(1)}, u32[]{:S(2)}) copy-start(bf16[14,4,48,128]{3,0,2,1:T(8,128)(2,1)S(1)} %fusion.49) | copy-start | bytes 2064388
  108.9 10.3 %collective-permute-start.7 = (bf16[14,48,128]{2,0,1:T(8,128)(2,1)S(1)}, bf16[14,48,128]{2,0,1:T(8,128)(2,1)S(1)}, u32[]{:S(2)}, u32[]{:S(2)}) collective-permute-start(bf16[14,48,128]{2,0,1:T(8,128)(2,1)S(1)} %get-tuple-element.10), channel_id=1, source_target_pairs={{0,8},{8,16},{16,24},{24,0},{1,9},{9,17},{17,25},{25,1},{2,10},{10... | collective-permute-start | bytes 516104 | tf_op jit(solution)/shard_map/ppermute | solution.py:30
  113.4 11.0 %collective-permute-start.26 = (bf16[14,48,128]{2,0,1:T(8,128)(2,1)}, bf16[14,48,128]{2,0,1:T(8,128)(2,1)}, u32[]{:S(2)}, u32[]{:S(2)}) collective-permute-start(bf16[14,48,128]{2,0,1:T(8,128)(2,1)} %fusion.52), channel_id=1, source_target_pairs={{0,8},{8,16},{16,24},{24,0},{1,9},{9,17},{17,25},{25,1},{2,10},{10... | collective-permute-start | bytes 516104 | tf_op jit(solution)/shard_map/ppermute | solution.py:30
  116.8 8.6 %collective-permute-start.9 = (bf16[14,48,128]{2,0,1:T(8,128)(2,1)}, bf16[14,48,128]{2,0,1:T(8,128)(2,1)}, u32[]{:S(2)}, u32[]{:S(2)}) collective-permute-start(bf16[14,48,128]{2,0,1:T(8,128)(2,1)} %get-tuple-element.11), channel_id=1, source_target_pairs={{0,24},{8,0},{16,8},{24,16},{1,25},{9,1},{17,9},{25,17},{2,26},{10... | collective-permute-start | bytes 516104 | tf_op jit(solution)/shard_map/ppermute | solution.py:30
  120.0 9.2 %collective-permute-start.8 = (bf16[14,48,128]{2,0,1:T(8,128)(2,1)}, bf16[14,48,128]{2,0,1:T(8,128)(2,1)}, u32[]{:S(2)}, u32[]{:S(2)}) collective-permute-start(bf16[14,48,128]{2,0,1:T(8,128)(2,1)} %fusion.58), channel_id=1, source_target_pairs={{0,8},{8,16},{16,24},{24,0},{1,9},{9,17},{17,25},{25,1},{2,10},{10... | collective-permute-start | bytes 516104 | tf_op jit(solution)/shard_map/ppermute | solution.py:30
  131.5 13.8 %collective-permute-start.29 = (bf16[14,48,128]{2,0,1:T(8,128)(2,1)}, bf16[14,48,128]{2,0,1:T(8,128)(2,1)S(1)}, u32[]{:S(2)}, u32[]{:S(2)}) collective-permute-start(bf16[14,48,128]{2,0,1:T(8,128)(2,1)} %get-tuple-element.8), channel_id=1, source_target_pairs={{0,8},{8,16},{16,24},{24,0},{1,9},{9,17},{17,25},{25,1},{2,10},{10... | collective-permute-start | bytes 516104 | tf_op jit(solution)/shard_map/ppermute | solution.py:30
  134.0 13.3 %collective-permute-start.32 = (bf16[14,48,128]{2,0,1:T(8,128)(2,1)}, bf16[14,48,128]{2,0,1:T(8,128)(2,1)S(1)}, u32[]{:S(2)}, u32[]{:S(2)}) collective-permute-start(bf16[14,48,128]{2,0,1:T(8,128)(2,1)} %get-tuple-element.9), channel_id=1, source_target_pairs={{0,8},{8,16},{16,24},{24,0},{1,9},{9,17},{17,25},{25,1},{2,10},{10... | collective-permute-start | bytes 516104 | tf_op jit(solution)/shard_map/ppermute | solution.py:30
  137.7 13.0 %collective-permute-start.28 = (bf16[14,48,128]{2,0,1:T(8,128)(2,1)}, bf16[14,48,128]{2,0,1:T(8,128)(2,1)}, u32[]{:S(2)}, u32[]{:S(2)}) collective-permute-start(bf16[14,48,128]{2,0,1:T(8,128)(2,1)} %get-tuple-element.8), channel_id=1, source_target_pairs={{0,24},{8,0},{16,8},{24,16},{1,25},{9,1},{17,9},{25,17},{2,26},{10... | collective-permute-start | bytes 516104 | tf_op jit(solution)/shard_map/ppermute | solution.py:30
  140.2 10.4 %collective-permute-start.31 = (bf16[14,48,128]{2,0,1:T(8,128)(2,1)}, bf16[14,48,128]{2,0,1:T(8,128)(2,1)S(1)}, u32[]{:S(2)}, u32[]{:S(2)}) collective-permute-start(bf16[14,48,128]{2,0,1:T(8,128)(2,1)} %get-tuple-element.9), channel_id=1, source_target_pairs={{0,24},{8,0},{16,8},{24,16},{1,25},{9,1},{17,9},{25,17},{2,26},{10... | collective-permute-start | bytes 516104 | tf_op jit(solution)/shard_map/ppermute | solution.py:30
  145.4 8.6 %collective-permute-start.30 = (bf16[14,48,128]{2,0,1:T(8,128)(2,1)S(1)}, bf16[14,48,128]{2,0,1:T(8,128)(2,1)S(1)}, u32[]{:S(2)}, u32[]{:S(2)}) collective-permute-start(bf16[14,48,128]{2,0,1:T(8,128)(2,1)S(1)} %collective-permute-done.29), channel_id=1, source_target_pairs={{0,8},{8,16},{16,24},{24,0},{1,9},{9,17},{17,25},{25,1},{2,10},{10... | collective-permute-start | bytes 516104 | tf_op jit(solution)/shard_map/ppermute | solution.py:30
  147.3 8.8 %collective-permute-start.33 = (bf16[14,48,128]{2,0,1:T(8,128)(2,1)S(1)}, bf16[14,48,128]{2,0,1:T(8,128)(2,1)S(1)}, u32[]{:S(2)}, u32[]{:S(2)}) collective-permute-start(bf16[14,48,128]{2,0,1:T(8,128)(2,1)S(1)} %collective-permute-done.32), channel_id=1, source_target_pairs={{0,8},{8,16},{16,24},{24,0},{1,9},{9,17},{17,25},{25,1},{2,10},{10... | collective-permute-start | bytes 516104 | tf_op jit(solution)/shard_map/ppermute | solution.py:30
  150.7 5.4 %copy-start.10 = (bf16[14,48,128]{2,0,1:T(8,128)(2,1)}, bf16[14,48,128]{2,0,1:T(8,128)(2,1)S(1)}, u32[]{:S(2)}) copy-start(bf16[14,48,128]{2,0,1:T(8,128)(2,1)S(1)} %collective-permute-done.31) | copy-start | bytes 516100
  165.0 148.9 %reduce-scatter.3.cloned.1.call-start = ((), (), s32[]{:S(2)}) async-start(), calls=%async_computation.3 | async-start | bytes 1671168 | tf_op jit(solution)/shard_map/reduce_scatter | solution.py:135
  177.6 3.5 %collective-permute-start.34 = (bf16[8,24,128]{2,0,1:T(8,128)(2,1)S(1)}, bf16[8,24,128]{2,0,1:T(8,128)(2,1)S(1)}, u32[]{:S(2)}, u32[]{:S(2)}) collective-permute-start(bf16[8,24,128]{2,0,1:T(8,128)(2,1)S(1)} %get-tuple-element.16), channel_id=1, source_target_pairs={{0,1},{1,2},{2,3},{3,4},{4,5},{5,6},{6,7},{7,0},{8,9},{9,10},{10,1... | collective-permute-start | bytes 147464 | tf_op jit(solution)/shard_map/ppermute | solution.py:30
  181.2 3.5 %collective-permute-start.35 = (bf16[8,24,128]{2,0,1:T(8,128)(2,1)S(1)}, bf16[8,24,128]{2,0,1:T(8,128)(2,1)S(1)}, u32[]{:S(2)}, u32[]{:S(2)}) collective-permute-start(bf16[8,24,128]{2,0,1:T(8,128)(2,1)S(1)} %fusion.67), channel_id=1, source_target_pairs={{0,1},{1,2},{2,3},{3,4},{4,5},{5,6},{6,7},{7,0},{8,9},{9,10},{10,1... | collective-permute-start | bytes 147464 | tf_op jit(solution)/shard_map/ppermute | solution.py:30
  183.7 4.8 %collective-permute-start.38 = (bf16[8,24,128]{2,0,1:T(8,128)(2,1)S(1)}, bf16[8,24,128]{2,0,1:T(8,128)(2,1)S(1)}, u32[]{:S(2)}, u32[]{:S(2)}) collective-permute-start(bf16[8,24,128]{2,0,1:T(8,128)(2,1)S(1)} %get-tuple-element.17), channel_id=1, source_target_pairs={{0,7},{1,0},{2,1},{3,2},{4,3},{5,4},{6,5},{7,6},{8,15},{9,8},{10,9... | collective-permute-start | bytes 147464 | tf_op jit(solution)/shard_map/ppermute | solution.py:30
  184.7 4.7 %collective-permute-start.36 = (bf16[8,24,128]{2,0,1:T(8,128)(2,1)S(1)}, bf16[8,24,128]{2,0,1:T(8,128)(2,1)S(1)}, u32[]{:S(2)}, u32[]{:S(2)}) collective-permute-start(bf16[8,24,128]{2,0,1:T(8,128)(2,1)S(1)} %fusion.66), channel_id=1, source_target_pairs={{0,1},{1,2},{2,3},{3,4},{4,5},{5,6},{6,7},{7,0},{8,9},{9,10},{10,1... | collective-permute-start | bytes 147464 | tf_op jit(solution)/shard_map/ppermute | solution.py:30
  189.4 4.6 %collective-permute-start.39 = (bf16[8,24,128]{2,0,1:T(8,128)(2,1)S(1)}, bf16[8,24,128]{2,0,1:T(8,128)(2,1)S(1)}, u32[]{:S(2)}, u32[]{:S(2)}) collective-permute-start(bf16[8,24,128]{2,0,1:T(8,128)(2,1)S(1)} %get-tuple-element.15), channel_id=1, source_target_pairs={{0,7},{1,0},{2,1},{3,2},{4,3},{5,4},{6,5},{7,6},{8,15},{9,8},{10,9... | collective-permute-start | bytes 147464 | tf_op jit(solution)/shard_map/ppermute | solution.py:30
  189.4 4.7 %collective-permute-start.37 = (bf16[8,24,128]{2,0,1:T(8,128)(2,1)S(1)}, bf16[8,24,128]{2,0,1:T(8,128)(2,1)S(1)}, u32[]{:S(2)}, u32[]{:S(2)}) collective-permute-start(bf16[8,24,128]{2,0,1:T(8,128)(2,1)S(1)} %get-tuple-element.14), channel_id=1, source_target_pairs={{0,1},{1,2},{2,3},{3,4},{4,5},{5,6},{6,7},{7,0},{8,9},{9,10},{10,1... | collective-permute-start | bytes 147464 | tf_op jit(solution)/shard_map/ppermute | solution.py:30
  194.0 5.3 %collective-permute-start.40 = (bf16[8,24,128]{2,0,1:T(8,128)(2,1)S(1)}, bf16[8,24,128]{2,0,1:T(8,128)(2,1)S(1)}, u32[]{:S(2)}, u32[]{:S(2)}) collective-permute-start(bf16[8,24,128]{2,0,1:T(8,128)(2,1)S(1)} %fusion.61), channel_id=1, source_target_pairs={{0,7},{1,0},{2,1},{3,2},{4,3},{5,4},{6,5},{7,6},{8,15},{9,8},{10,9... | collective-permute-start | bytes 147464 | tf_op jit(solution)/shard_map/ppermute | solution.py:30
  (10 other events, 20.8 us)
Sparse Core Ops, SparseCore 0:
  21.2 71.5 all-gather.1
  165.1 75.3 reduce-scatter.4
  243.4 70.4 reduce-scatter.2
